TPU v7x, 512 devices: a whole 4x8x8 slice. The times are simulated.
512 devices in a mesh: segment: 4 (over z_lo), seq: 16 (over z_hi, x, core), mp: 8 (over y).
Axes of the slice: x: 4, y: 8, z: 8 (z_hi: 2, z_lo: 4; z = z_hi * 4 + z_lo), core: 2. Of those that a mesh axis runs over, the one named last changes fastest.
Arguments:
- latents: bfloat16 [4, 16, 256, 4096], P('segment', 'seq', None, 'mp'), may hold values from -6 to 6
- w_qkv: bfloat16 [4, 4096, 3, 4096], P('segment', 'seq', None, 'mp'), may hold values from -1 to 1
- w_out: bfloat16 [4, 4096, 4096], P('segment', 'mp', 'seq'), may hold values from -0.09375 to 0.09375
- mod_shift: float32 [4, 4096], P('segment'), may hold values from -3 to 3
- mod_scale: float32 [4, 4096], P('segment'), may hold values from 0.1 to 1.9
- mod_gate: float32 [4, 4096], P('segment'), may hold values from 0.5 to 1.5
- counts: int32 [4, 16], P('segment'), may hold values from 64 to 256, as said below
Outputs:
- next_latents: bfloat16 [4, 16, 256, 4096], P('segment', 'seq', None, 'mp')
Inputs may be any that keep to these rules, and one draw needn't show every extreme that they name: `counts`: in every section's clip at least one frame has all 256 patch positions valid.
All inputs are finite; a program needn't handle non-finite values.
Results may differ from a plain program's by a relative error of at most 0.01.
Values may be sent and summed in bfloat16 or wider, within the bound.
No kernel may reach another device: no remote copies, remote signals or barrier semaphores. Data moves between devices by JAX's collectives and lax.ppermute only.
A program may use at most 64 MiB of HBM per device.

v0:
```python
import math

import jax
import jax.numpy as jnp
from jax import lax
from jax.sharding import PartitionSpec as P

HD = 128


EPS = 1e-06
NEG_FILL = -1e30


def passed_along(x, axis, by):
    length = lax.axis_size(axis)
    return lax.ppermute(x, axis, [(i, (i + by) % length) for i in range(length)])


def masked_attention(queries, keys_in, values, usable):
    factor = 1.0 / math.sqrt(queries.shape[-1])
    scores = (
        jnp.einsum("...ihe,...jhe->...hij", queries, keys_in, preferred_element_type=jnp.float32)
        * factor
    )
    allowed = usable[..., None, :, None] & usable[..., None, None, :]
    masked = jnp.where(allowed, scores, NEG_FILL)
    highest = jnp.max(masked, axis=-1, keepdims=True)
    raised = jnp.where(allowed, jnp.exp(masked - highest), 0.0)
    spare_one = jnp.where(usable, 0.0, 1.0)[..., None, :, None]
    weights = (raised / (jnp.sum(raised, axis=-1, keepdims=True) + spare_one)).astype(jnp.bfloat16)
    blended = jnp.einsum(
        "...hij,...jhe->...ihe", weights, values, preferred_element_type=jnp.float32
    )
    return blended.astype(jnp.bfloat16)


def relay_features(rows_now):
    return lax.all_to_all(rows_now, "seq", split_axis=0, concat_axis=0, tiled=True)


def pass_onward(rows_now):
    return passed_along(rows_now, "segment", 1)


def on_device(latents, w_qkv, w_out, mod_shift, mod_scale, mod_gate, counts):
    frames = lax.axis_size("seq")
    patches = latents.shape[2]
    narrow = latents.shape[3]
    span = patches // frames
    segment_rows = latents[0, 0]
    gathered = lax.all_gather(latents, "mp", axis=3, tiled=True)[0, 0]
    widened = gathered.astype(jnp.float32)
    average = jnp.mean(widened, axis=-1, keepdims=True)
    centred = widened - average
    variance = jnp.mean(centred * centred, axis=-1, keepdims=True)
    modulated = (centred * lax.rsqrt(variance + EPS) * mod_scale[0] + mod_shift[0]).astype(
        jnp.bfloat16
    )
    columns = w_qkv.shape[2] * w_qkv.shape[3]
    piece = lax.all_gather(w_qkv, "seq", axis=1, tiled=True)
    height = piece.shape[1]
    projected = jnp.dot(
        modulated, piece.reshape(height, columns), preferred_element_type=jnp.float32
    )
    local_heads = w_qkv.shape[3] // HD
    projected = projected.astype(jnp.bfloat16).reshape(patches, 3, local_heads, HD)
    frame_here = lax.axis_index("seq")
    clip_counts = counts[0]
    positions = jnp.arange(frames)

    def spatial(triple):
        count_here = jnp.sum(jnp.where(positions == frame_here, clip_counts, 0))
        usable = jnp.arange(patches) < count_here
        return masked_attention(triple[:, 0], triple[:, 1], triple[:, 2], usable)

    def temporal(triple):
        by_place = triple.reshape(frames, span, 3, local_heads, HD).transpose(1, 0, 2, 3, 4)
        location = frame_here * span + jnp.arange(span)
        usable = location[:, None] < clip_counts[None, :]
        blended = masked_attention(by_place[:, :, 0], by_place[:, :, 1], by_place[:, :, 2], usable)
        return blended.transpose(1, 0, 2, 3).reshape(patches, local_heads, HD)

    attended = lax.cond(lax.axis_index("segment") % 2 == 0, spatial, temporal, projected)
    attended = attended.reshape(patches, local_heads * HD)
    out_whole = lax.all_gather(w_out, "seq", axis=2, tiled=True)[0]
    member = lax.axis_index("mp")
    partials = jnp.dot(attended, out_whole, preferred_element_type=jnp.float32)
    summed = lax.psum_scatter(
        partials.astype(jnp.bfloat16), "mp", scatter_dimension=1, tiled=True
    ).astype(jnp.float32)
    gate_here = lax.dynamic_slice_in_dim(mod_gate[0], member * narrow, narrow)
    updated = (segment_rows.astype(jnp.float32) + gate_here * summed).astype(jnp.bfloat16)
    updated = updated.reshape(frames, span, narrow)
    moved = pass_onward(relay_features(updated))
    return moved.reshape(1, 1, patches, narrow)


def solution(mesh):
    return jax.shard_map(
        on_device,
        mesh=mesh,
        in_specs=(
            P("segment", "seq", None, "mp"),
            P("segment", "seq", None, "mp"),
            P("segment", "mp", "seq"),
            P("segment", None),
            P("segment", None),
            P("segment", None),
            P("segment", None),
        ),
        out_specs=P("segment", "seq", None, "mp"),
        check_vma=False,
    )
```

profile of v0, /device:TPU:1, one launch (start us, length us, event | category | flops | bytes accessed | tf_op | source)
XLA Modules:
  0.0 384.6 jit_solution(8186895898152812026)
XLA Ops:
  6.5 0.0 copy-start
  6.5 0.0 copy-start.5
  6.5 0.0 copy-start.4
  6.5 0.0 all-gather.4.cloned.1.call-start
  6.5 0.7 all-gather.4.cloned.1.call-update
  7.3 0.0 all-gather.6.cloned.1.call-start
  7.3 2.3 copy.18
  9.6 0.0 all-gather.6.cloned.1.call-update
  9.7 0.0 all-gather.8.cloned.1.call-start
  9.7 0.7 all-gather.8.cloned.1.call-update
  10.4 0.0 reduce-scatter.2.cloned.1.call-start
  10.5 43.7 %all-gather.4.cloned.1.call-done = bf16[1,1,256,4096]{3,2,1,0:T(8,128)(2,1)} async-done(((bf16[1,1,256,512]{3,2,1,0:T(8,128)(2,1)}), bf16[1,1,256,4096]{3,2,1,0:T(8,128)(2,1)}) %all-gather.4.cloned.1.call-update) | async-done | bytes 2097168 | tf_op jit(solution)/shard_map/all_gather | solution.py:52
  54.1 0.0 copy-start.1
  54.1 2.1 convert_reduce_fusion
  56.2 2.3 fusion.30
  58.5 157.1 %all-gather.6.cloned.1.call-done = bf16[1,4096,3,512]{1,3,2,0:T(8,128)(2,1)} async-done(((bf16[1,256,3,512]{1,3,2,0:T(8,128)(2,1)}), bf16[1,4096,3,512]{1,3,2,0:T(8,128)(2,1)}) %all-gather.6.cloned.1.call-update) | async-done | bytes 12582928 | tf_op jit(solution)/shard_map/all_gather | solution.py:61
  215.6 0.0 copy-done.5
  215.6 0.0 copy-done.4
  215.6 0.0 copy-done.1
  215.7 0.0 copy-start.3
  215.7 8.2 %convolution_convert_fusion.3 = bf16[256,1536]{1,0:T(8,128)(2,1)S(1)} fusion(bf16[4096,1536]{0,1:T(8,128)(2,1)} %bitcast.96, bf16[1,1,256,4096]{3,2,1,0:T(8,128)(2,1)S(1)} %copy-done.1, f32[4096]{0:T(1024)S(1)} %bitcast.97, f32[4096]{0:T(1024)S(1)} %bitcast.98, f32[256]{0:T(256)S(1)} %add_rsqrt_fusion, f32[256]{0:T(256)S(1)} %broadcast_multiply_fusion), kind=kOutput, calls=%fused_computation.58 | convolution fusion | flops 3227910144 | bytes 15501312 | tf_op jit(solution)/shard_map/dot_general | solution.py:63
  223.9 0.0 copy-done.3
  223.9 3.7 conditional.1
  223.9 0.6 fusion.14
  224.6 0.6 iota_compare_fusion
  225.1 0.1 broadcast_and_fusion.1
  225.2 0.3 copy.19
  225.5 0.6 fusion.40
  226.2 0.6 broadcast_select_fusion.1
  226.7 0.8 convolution_convert_fusion.1
  227.6 0.0 copy-start.2
  227.6 71.0 %all-gather.8.cloned.1.call-done = bf16[1,512,4096]{2,1,0:T(8,128)(2,1)} async-done(((bf16[1,512,256]{2,1,0:T(8,128)(2,1)}), bf16[1,512,4096]{2,1,0:T(8,128)(2,1)}) %all-gather.8.cloned.1.call-update) | async-done | bytes 4194320 | tf_op jit(solution)/shard_map/all_gather | solution.py:86
  298.5 4.8 %convolution_convert_fusion.2 = bf16[256,4096]{1,0:T(8,128)(2,1)} fusion(bf16[256,512]{0,1:T(8,128)(2,1)S(1)} %get-tuple-element.36, bf16[1,512,4096]{2,1,0:T(8,128)(2,1)} %all-gather.8.cloned.1.call-done), kind=kOutput, calls=%fused_computation.49 | convolution fusion | flops 1074790400 | bytes 6553600 | tf_op jit(solution)/shard_map/dot_general | solution.py:88
  303.4 0.0 reduce-scatter.2.cloned.1.call-update
  303.4 0.0 copy-done
  303.4 36.3 %reduce-scatter.2.cloned.1.call-done = bf16[256,512]{1,0:T(8,128)(2,1)} async-done(((bf16[256,4096]{1,0:T(8,128)(2,1)}), bf16[256,512]{1,0:T(8,128)(2,1)}) %reduce-scatter.2.cloned.1.call-update) | async-done | bytes 262160 | tf_op jit(solution)/shard_map/reduce_scatter | solution.py:89
  339.7 0.0 copy-done.2
  339.7 1.0 fusion.38
  340.7 26.0 %all_to_all.5 = bf16[16,16,512]{2,1,0:T(8,128)(2,1)S(1)} all-to-all(bf16[16,16,512]{2,1,0:T(8,128)(2,1)S(1)} %bitcast.84), channel_id=1, replica_groups=mesh['segment'=4,'seq'=16,'mp'=8] {'seq'}, dimensions={0} | all-to-all | bytes 524288 | tf_op jit(solution)/shard_map/all_to_all | solution.py:39
  366.8 5.0 %collective-permute-start = (bf16[16,16,512]{2,1,0:T(8,128)(2,1)S(1)}, bf16[16,16,512]{2,1,0:T(8,128)(2,1)S(1)}, u32[]{:S(2)}, u32[]{:S(2)}) collective-permute-start(bf16[16,16,512]{2,1,0:T(8,128)(2,1)S(1)} %all_to_all.5), channel_id=1, source_target_pairs={{0,128},{128,256},{256,384},{384,0},{1,129},{129,257},{257,385},{3... | collective-permute-start | bytes 786440 | tf_op jit(solution)/shard_map/ppermute | solution.py:17
  371.7 5.6 %collective-permute-done = bf16[16,16,512]{2,1,0:T(8,128)(2,1)S(1)} collective-permute-done((bf16[16,16,512]{2,1,0:T(8,128)(2,1)S(1)}, bf16[16,16,512]{2,1,0:T(8,128)(2,1)S(1)}, u32[]{:S(2)}, u32[]{:S(2)}) %collective-permute-start) | collective-permute-done | bytes 262176 | tf_op jit(solution)/shard_map/ppermute | solution.py:17
  377.4 0.7 copy.32
  (5 shorter events, 0.0 us)
Async XLA Ops:
  6.5 296.9 %copy-start = (f32[1,4096]{1,0:T(1,128)S(1)}, f32[1,4096]{1,0:T(1,128)}, u32[]{:S(2)}) copy-start(f32[1,4096]{1,0:T(1,128)} %param.14) | copy-start | bytes 49156
  6.5 209.1 %copy-start.5 = (f32[1,4096]{1,0:T(1,128)S(1)}, f32[1,4096]{1,0:T(1,128)}, u32[]{:S(2)}) copy-start(f32[1,4096]{1,0:T(1,128)} %param.13) | copy-start | bytes 49156
  6.5 209.1 %copy-start.4 = (f32[1,4096]{1,0:T(1,128)S(1)}, f32[1,4096]{1,0:T(1,128)}, u32[]{:S(2)}) copy-start(f32[1,4096]{1,0:T(1,128)} %param.12) | copy-start | bytes 49156
  6.5 47.6 %all-gather.4.cloned.1.call-start = ((), (), s32[]{:S(2)}) async-start(), calls=%async_computation.2 | async-start | bytes 2359296 | tf_op jit(solution)/shard_map/all_gather | solution.py:52
  7.3 208.4 %all-gather.6.cloned.1.call-start = ((), (), s32[]{:S(2)}) async-start(), calls=%async_computation.3 | async-start | bytes 13369344 | tf_op jit(solution)/shard_map/all_gather | solution.py:61
  9.7 288.9 %all-gather.8.cloned.1.call-start = ((), (), s32[]{:S(2)}) async-start(), calls=%async_computation.4 | async-start | bytes 4456448 | tf_op jit(solution)/shard_map/all_gather | solution.py:86
  10.4 329.3 %reduce-scatter.2.cloned.1.call-start = ((), (), s32[]{:S(2)}) async-start(), calls=%async_computation.5 | async-start | bytes 2359296 | tf_op jit(solution)/shard_map/reduce_scatter | solution.py:89
  54.1 161.5 %copy-start.1 = (bf16[1,1,256,4096]{3,2,1,0:T(8,128)(2,1)S(1)}, bf16[1,1,256,4096]{3,2,1,0:T(8,128)(2,1)}, u32[]{:S(2)}) copy-start(bf16[1,1,256,4096]{3,2,1,0:T(8,128)(2,1)} %all-gather.4.cloned.1.call-done) | copy-start | bytes 6291460
  215.7 8.3 %copy-start.3 = (s32[1,16]{1,0:T(1,128)S(1)}, s32[1,16]{1,0:T(1,128)}, u32[]{:S(2)}) copy-start(s32[1,16]{1,0:T(1,128)} %param.15) | copy-start | bytes 196
  227.6 112.1 %copy-start.2 = (bf16[1,1,256,512]{3,2,1,0:T(8,128)(2,1)S(1)}, bf16[1,1,256,512]{3,2,1,0:T(8,128)(2,1)}, u32[]{:S(2)}) copy-start(bf16[1,1,256,512]{3,2,1,0:T(8,128)(2,1)} %param.9) | copy-start | bytes 786436
  366.8 10.6 %collective-permute-start = (bf16[16,16,512]{2,1,0:T(8,128)(2,1)S(1)}, bf16[16,16,512]{2,1,0:T(8,128)(2,1)S(1)}, u32[]{:S(2)}, u32[]{:S(2)}) collective-permute-start(bf16[16,16,512]{2,1,0:T(8,128)(2,1)S(1)} %all_to_all.5), channel_id=1, source_target_pairs={{0,128},{128,256},{256,384},{384,0},{1,129},{129,257},{257,385},{3... | collective-permute-start | bytes 786440 | tf_op jit(solution)/shard_map/ppermute | solution.py:17
Sparse Core Ops, SparseCore 0:
  9.4 44.6 all-gather.3
  57.3 158.3 all-gather.5
  218.8 79.7 all-gather.7
  303.5 36.1 reduce-scatter.1
where the time goes:
time: 385 us
  waiting for transfers between devices  315 us (82%)
  blocking collectives  26 us (7%)
  matrix products  14.5 us (4%)
  between operations  13.2 us (3%)
  other arithmetic  7.29 us (2%)
  starting transfers between devices  5.07 us (1%)
    all_gather x1, waiting for transfers between devices, on_device(): piece = lax.all_gather(w_qkv, 'seq', axis=1, tiled=True)  157 us
    all_gather x1, waiting for transfers between devices, on_device(): out_whole = lax.all_gather(w_out, 'seq', axis=2, tiled=True)[0]  71 us
    all_gather x1, waiting for transfers between devices, on_device(): gathered = lax.all_gather(latents, 'mp', axis=3, tiled=True)[0, 0]  43.7 us
    reduce_scatter x1, waiting for transfers between devices, on_device(): lax.psum_scatter(partials.astype(jnp.bfloat16), 'mp', scatter_dimension=1...  36.3 us
    all_to_all x1, blocking collectives, relay_features(): lax.all_to_all(rows_now, 'seq', split_axis=0, concat_axis=0, tiled=True)  26 us
    dot_general x1, matrix products, on_device(): jnp.dot(modulated, piece.reshape(height, columns), preferred_element_type...  8.22 us
  transfers between devices with their start and end apart: 5, of which 5 were waited for; matrix products, arithmetic and copies ran while one was open for 5% of the time, Pallas kernels for 0%

commit v1 on v0

--- a/solution.py
+++ b/solution.py
@@ -35,8 +35,24 @@
     return blended.astype(jnp.bfloat16)
 
 
+SEQ = ("zh", "x", "c")
+
+
+def seq_index():
+    return (lax.axis_index("zh") * lax.axis_size("x") + lax.axis_index("x")) * lax.axis_size(
+        "c"
+    ) + lax.axis_index("c")
+
+
+def gather_seq(block):
+    across = lax.all_gather(block, "zh", axis=0)
+    along = lax.all_gather(across, "x", axis=1)
+    both = lax.all_gather(along, "c", axis=2)
+    return both.reshape((-1,) + block.shape[1:])
+
+
 def relay_features(rows_now):
-    return lax.all_to_all(rows_now, "seq", split_axis=0, concat_axis=0, tiled=True)
+    return lax.all_to_all(rows_now, SEQ, split_axis=0, concat_axis=0, tiled=True)
 
 
 def pass_onward(rows_now):
@@ -44,7 +60,7 @@
 
 
 def on_device(latents, w_qkv, w_out, mod_shift, mod_scale, mod_gate, counts):
-    frames = lax.axis_size("seq")
+    frames = lax.axis_size(SEQ)
     patches = latents.shape[2]
     narrow = latents.shape[3]
     span = patches // frames
@@ -58,14 +74,14 @@
         jnp.bfloat16
     )
     columns = w_qkv.shape[2] * w_qkv.shape[3]
-    piece = lax.all_gather(w_qkv, "seq", axis=1, tiled=True)
-    height = piece.shape[1]
+    piece = gather_seq(w_qkv[0])
+    height = piece.shape[0]
     projected = jnp.dot(
         modulated, piece.reshape(height, columns), preferred_element_type=jnp.float32
     )
     local_heads = w_qkv.shape[3] // HD
     projected = projected.astype(jnp.bfloat16).reshape(patches, 3, local_heads, HD)
-    frame_here = lax.axis_index("seq")
+    frame_here = seq_index()
     clip_counts = counts[0]
     positions = jnp.arange(frames)
 
@@ -83,9 +99,11 @@
 
     attended = lax.cond(lax.axis_index("segment") % 2 == 0, spatial, temporal, projected)
     attended = attended.reshape(patches, local_heads * HD)
-    out_whole = lax.all_gather(w_out, "seq", axis=2, tiled=True)[0]
+    out_blocks = gather_seq(w_out[0][None])
     member = lax.axis_index("mp")
-    partials = jnp.dot(attended, out_whole, preferred_element_type=jnp.float32)
+    partials = jnp.einsum(
+        "tr,brc->tbc", attended, out_blocks, preferred_element_type=jnp.float32
+    ).reshape(patches, -1)
     summed = lax.psum_scatter(
         partials.astype(jnp.bfloat16), "mp", scatter_dimension=1, tiled=True
     ).astype(jnp.float32)
@@ -97,18 +115,21 @@
 
 
 def solution(mesh):
+    seg, seq, mp = mesh.devices.shape
+    inner = mesh.devices.reshape(seg, 2, seq // 4, 2, mp)
+    fine = jax.sharding.Mesh(inner, ("segment", "zh", "x", "c", "mp"))
     return jax.shard_map(
         on_device,
-        mesh=mesh,
+        mesh=fine,
         in_specs=(
-            P("segment", "seq", None, "mp"),
-            P("segment", "seq", None, "mp"),
-            P("segment", "mp", "seq"),
+            P("segment", SEQ, None, "mp"),
+            P("segment", SEQ, None, "mp"),
+            P("segment", "mp", SEQ),
             P("segment", None),
             P("segment", None),
             P("segment", None),
             P("segment", None),
         ),
-        out_specs=P("segment", "seq", None, "mp"),
+        out_specs=P("segment", SEQ, None, "mp"),
         check_vma=False,
     )

time: 385 us -> 411 us (1.068)
  local copies, waits for them, and re-layouts: 3.33 us -> 39.8 us
  waiting for transfers between devices: 315 us -> 284 us
  blocking collectives: 26 us -> 45.2 us
    all_gather x2 -> x5, waiting for transfers between devices: 228 us -> 205 us  [the longest x2 107 us: gather_seq(): along = lax.all_gather(across, 'x', axis=1)]
    another operation x1 -> x2, local copies, waits for them, and re-layouts: 0.27 us -> 21.3 us  [the longest x1 21 us: on_device(): piece.reshape(height, columns)]
    all_gather x0 -> x1, blocking collectives: none -> 19.6 us  [gather_seq(): across = lax.all_gather(block, 'zh', axis=0)]
    all_gather x1, waiting for transfers between devices: 43.7 us -> 30.5 us  [on_device(): gathered = lax.all_gather(latents, 'mp', axis=3, tiled=True)[0, 0]]
    all_gather x0 -> x1, local copies, waits for them, and re-layouts: none -> 11.4 us  [gather_seq(): along = lax.all_gather(across, 'x', axis=1)]
    dot_general x0 -> x1, local copies, waits for them, and re-layouts: none -> 6.38 us  [on_device(): jnp.einsum('tr,brc->tbc', attended, out_blocks, preferred_element_type=jn...]
    reduce_scatter x1, waiting for transfers between devices: 36.3 us -> 40.9 us  [on_device(): lax.psum_scatter(partials.astype(jnp.bfloat16), 'mp', scatter_dimension=1...]
  transfers between devices with their start and end apart: 5 -> 8, of which waited for: 5 -> 8; matrix products, arithmetic and copies ran while one was open for 5% -> 5% of each run, Pallas kernels for 0% -> 0%
where the time goes in v1:
time: 411 us; the launch traced here: 409 us
  waiting for transfers between devices  284 us (69%)
  blocking collectives  45.2 us (11%)
  local copies, waits for them, and re-layouts  39.8 us (10%)
  matrix products  14.4 us (4%)
  between operations  13.6 us (3%)
  other arithmetic  7.48 us (2%)
  starting transfers between devices  5.16 us (1%)
    all_gather x2, waiting for transfers between devices, gather_seq(): along = lax.all_gather(across, 'x', axis=1)  107 us
    all_gather x2, waiting for transfers between devices, gather_seq(): both = lax.all_gather(along, 'c', axis=2)  53.6 us
    all_gather x1, waiting for transfers between devices, gather_seq(): across = lax.all_gather(block, 'zh', axis=0)  44.4 us
    reduce_scatter x1, waiting for transfers between devices, on_device(): lax.psum_scatter(partials.astype(jnp.bfloat16), 'mp', scatter_dimension=1...  40.9 us
    all_gather x1, waiting for transfers between devices, on_device(): gathered = lax.all_gather(latents, 'mp', axis=3, tiled=True)[0, 0]  30.5 us
    all_to_all x1, blocking collectives, relay_features(): lax.all_to_all(rows_now, SEQ, split_axis=0, concat_axis=0, tiled=True)  25.7 us
    another operation x1, local copies, waits for them, and re-layouts, on_device(): piece.reshape(height, columns)  21 us
    all_gather x1, blocking collectives, gather_seq(): across = lax.all_gather(block, 'zh', axis=0)  19.6 us
  transfers between devices with their start and end apart: 8, of which 8 were waited for; matrix products, arithmetic and copies ran while one was open for 5% of the time, Pallas kernels for 0%

profile of v1, /device:TPU:1, one launch (start us, length us, event | category | flops | bytes accessed | tf_op | source)
XLA Modules:
  0.0 409.4 jit_solution(5378004970461024760)
XLA Ops:
  6.5 0.0 copy-start
  6.5 0.0 all-gather.14.cloned.1.call-start
  6.5 0.7 all-gather.14.cloned.1.call-update
  7.3 0.0 all-gather.20.cloned.1.call-start
  7.3 19.6 %all-gather.2 = bf16[2,512,256]{2,1,0:T(8,128)(2,1)} all-gather(bf16[1,512,256]{2,1,0:T(8,128)(2,1)} %param.11), channel_id=4, replica_groups=mesh['segment'=4,'zh'=2,'x'=4,'c'=2,'mp'=8] {'zh'}, dimensions={0}, use_global_device_ids=true | all-gather | bytes 786432 | tf_op jit(solution)/shard_map/all_gather | solution.py:48
  26.9 0.0 all-gather.20.cloned.1.call-update
  26.9 0.0 all-gather.16.cloned.1.call-start
  26.9 44.4 %all-gather.14.cloned.1.call-done = bf16[2,256,3,512]{3,1,2,0:T(8,128)(2,1)} async-done(((bf16[1,256,3,512]{3,1,2,0:T(8,128)(2,1)}), bf16[2,256,3,512]{3,1,2,0:T(8,128)(2,1)}) %all-gather.14.cloned.1.call-update) | async-done | bytes 1572880 | tf_op jit(solution)/shard_map/all_gather | solution.py:48
  71.4 0.0 all-gather.16.cloned.1.call-update
  71.4 0.0 all-gather.12.cloned.1.call-start
  71.4 0.5 all-gather.12.cloned.1.call-update
  72.0 0.0 all-gather.22.cloned.1.call-start
  72.0 34.1 %all-gather.20.cloned.1.call-done = bf16[2,2048,256]{2,1,0:T(8,128)(2,1)} async-done(((bf16[2,512,256]{2,1,0:T(8,128)(2,1)}), bf16[2,2048,256]{2,1,0:T(8,128)(2,1)}) %all-gather.20.cloned.1.call-update) | async-done | bytes 2097168 | tf_op jit(solution)/shard_map/all_gather | solution.py:49
  106.1 0.0 all-gather.22.cloned.1.call-update
  106.2 0.0 all-gather.18.cloned.1.call-start
  106.2 73.1 %all-gather.16.cloned.1.call-done = bf16[2,1024,3,512]{3,1,2,0:T(8,128)(2,1)} async-done(((bf16[2,256,3,512]{3,1,2,0:T(8,128)(2,1)}), bf16[2,1024,3,512]{3,1,2,0:T(8,128)(2,1)}) %all-gather.16.cloned.1.call-update) | async-done | bytes 6291472 | tf_op jit(solution)/shard_map/all_gather | solution.py:49
  179.3 11.4 %copy.28 = bf16[2,4,256,3,512]{2,1,0,4,3:T(4,128)(2,1)} copy(bf16[2,4,256,3,512]{4,2,1,3,0:T(8,128)(2,1)} %bitcast.90) | data formatting | bytes 12582912 | tf_op jit(solution)/shard_map/all_gather | solution.py:49
  190.8 0.0 all-gather.18.cloned.1.call-update
  190.8 0.0 reduce-scatter.2.cloned.1.call-start
  190.8 30.5 %all-gather.12.cloned.1.call-done = bf16[1,1,256,4096]{3,2,1,0:T(8,128)(2,1)} async-done(((bf16[1,1,256,512]{3,2,1,0:T(8,128)(2,1)}), bf16[1,1,256,4096]{3,2,1,0:T(8,128)(2,1)}) %all-gather.12.cloned.1.call-update) | async-done | bytes 2097168 | tf_op jit(solution)/shard_map/all_gather | solution.py:68
  221.4 2.0 convert_reduce_fusion
  223.3 2.3 fusion.30
  225.6 23.9 %all-gather.22.cloned.1.call-done = bf16[2,4,2,512,256]{4,3,2,1,0:T(8,128)(2,1)} async-done(((bf16[2,4,1,512,256]{4,3,2,1,0:T(8,128)(2,1)}), bf16[2,4,2,512,256]{4,3,2,1,0:T(8,128)(2,1)}) %all-gather.22.cloned.1.call-update) | async-done | bytes 4194320 | tf_op jit(solution)/shard_map/all_gather | solution.py:50
  249.5 6.4 %copy.30 = bf16[16,256,512]{2,1,0:T(8,128)(2,1)} copy(bf16[16,256,512]{1,2,0:T(8,128)(2,1)} %bitcast.91) | data formatting | bytes 8388608 | tf_op jit(solution)/shard_map/tr,brc->tbc/dot_general | solution.py:104
  255.9 29.7 %all-gather.18.cloned.1.call-done = bf16[2,4,512,3,512]{2,1,0,4,3:T(4,128)(2,1)} async-done(((bf16[2,4,256,3,512]{2,1,0,4,3:T(4,128)(2,1)}), bf16[2,4,512,3,512]{2,1,0,4,3:T(4,128)(2,1)}) %all-gather.18.cloned.1.call-update) | async-done | bytes 12582928 | tf_op jit(solution)/shard_map/all_gather | solution.py:50
  285.6 21.0 %reshape_reshape.6 = bf16[4096,1536]{0,1:T(8,128)(2,1)} reshape(bf16[2,4,512,3,512]{2,1,0,4,3:T(4,128)(2,1)} %all-gather.18.cloned.1.call-done) | data formatting | bytes 25165824 | tf_op jit(solution)/shard_map/reshape;reshape | solution.py:80
  306.6 0.0 copy-done.1
  306.6 0.0 copy-done.4
  306.6 0.0 copy-start.3
  306.6 8.1 %convolution_convert_fusion.3 = bf16[256,1536]{1,0:T(8,128)(2,1)S(1)} fusion(bf16[4096,1536]{0,1:T(8,128)(2,1)} %reshape_reshape.6, bf16[1,1,256,4096]{3,2,1,0:T(8,128)(2,1)S(1)} %copy-done.1, f32[4096]{0:T(1024)S(1)} %bitcast.105, f32[4096]{0:T(1024)S(1)} %bitcast.106, f32[256]{0:T(256)S(1)} %add_rsqrt_fusion, f32[256]{0:T(256)S(1)} %broadcast_multiply_fusion), kind=kOutput, calls=%fused_computation.57 | convolution fusion | flops 3227910144 | bytes 15501312 | tf_op jit(solution)/shard_map/dot_general | solution.py:79
  314.7 4.0 conditional.1
  314.8 0.7 fusion.14
  315.5 0.3 copy.29
  315.7 0.7 iota_compare_fusion
  316.4 0.7 broadcast_select_fusion.1
  317.1 0.1 broadcast_and_fusion.1
  317.2 0.6 fusion.39
  317.9 0.8 convolution_convert_fusion.1
  318.7 0.0 copy-start.2
  318.7 4.9 %convolution_convert_fusion.2 = bf16[256,4096]{1,0:T(8,128)(2,1)} fusion(bf16[256,512]{0,1:T(8,128)(2,1)S(1)} %get-tuple-element.40, bf16[4096,512]{1,0:T(8,128)(2,1)} %bitcast.89), kind=kOutput, calls=%fused_computation.49 | convolution fusion | flops 1074790400 | bytes 6553600 | tf_op jit(solution)/shard_map/tr,brc->tbc/dot_general | solution.py:104
  323.6 0.0 reduce-scatter.2.cloned.1.call-update
  323.7 0.0 copy-done
  323.7 40.9 %reduce-scatter.2.cloned.1.call-done = bf16[256,512]{1,0:T(8,128)(2,1)} async-done(((bf16[256,4096]{1,0:T(8,128)(2,1)}), bf16[256,512]{1,0:T(8,128)(2,1)}) %reduce-scatter.2.cloned.1.call-update) | async-done | bytes 262160 | tf_op jit(solution)/shard_map/reduce_scatter | solution.py:107
  364.5 1.0 fusion.37
  365.6 25.7 %all_to_all.5 = bf16[16,16,512]{2,1,0:T(8,128)(2,1)S(1)} all-to-all(bf16[16,16,512]{2,1,0:T(8,128)(2,1)S(1)} %bitcast.93), channel_id=1, replica_groups=mesh['segment'=4,'zh'=2,'x'=4,'c'=2,'mp'=8] {'zh','x','c'}, dimensions={0} | all-to-all | bytes 524288 | tf_op jit(solution)/shard_map/all_to_all | solution.py:55
  391.2 4.9 %collective-permute-start = (bf16[16,16,512]{2,1,0:T(8,128)(2,1)S(1)}, bf16[16,16,512]{2,1,0:T(8,128)(2,1)S(1)}, u32[]{:S(2)}, u32[]{:S(2)}) collective-permute-start(bf16[16,16,512]{2,1,0:T(8,128)(2,1)S(1)} %all_to_all.5), channel_id=1, source_target_pairs={{0,128},{128,256},{256,384},{384,0},{1,129},{129,257},{257,385},{3... | collective-permute-start | bytes 786440 | tf_op jit(solution)/shard_map/ppermute | solution.py:17
  396.2 5.6 %collective-permute-done = bf16[16,16,512]{2,1,0:T(8,128)(2,1)S(1)} collective-permute-done((bf16[16,16,512]{2,1,0:T(8,128)(2,1)S(1)}, bf16[16,16,512]{2,1,0:T(8,128)(2,1)S(1)}, u32[]{:S(2)}, u32[]{:S(2)}) %collective-permute-start) | collective-permute-done | bytes 262176 | tf_op jit(solution)/shard_map/ppermute | solution.py:17
  401.8 0.7 copy.43
  (11 shorter events, 0.0 us)
Async XLA Ops:
  6.5 317.1 %copy-start = (f32[1,4096]{1,0:T(1,128)S(1)}, f32[1,4096]{1,0:T(1,128)}, u32[]{:S(2)}) copy-start(f32[1,4096]{1,0:T(1,128)} %param.14) | copy-start | bytes 49156
  6.5 64.8 %all-gather.14.cloned.1.call-start = ((), (), s32[]{:S(2)}) async-start(), calls=%async_computation.3 | async-start | bytes 2359296 | tf_op jit(solution)/shard_map/all_gather | solution.py:48
  7.3 98.9 %all-gather.20.cloned.1.call-start = ((), (), s32[]{:S(2)}) async-start(), calls=%async_computation.7 | async-start | bytes 2621440 | tf_op jit(solution)/shard_map/all_gather | solution.py:49
  26.9 152.4 %all-gather.16.cloned.1.call-start = ((), (), s32[]{:S(2)}) async-start(), calls=%async_computation.5 | async-start | bytes 7864320 | tf_op jit(solution)/shard_map/all_gather | solution.py:49
  71.4 150.0 %all-gather.12.cloned.1.call-start = ((), (), s32[]{:S(2)}) async-start(), calls=%async_computation.2 | async-start | bytes 2359296 | tf_op jit(solution)/shard_map/all_gather | solution.py:68
  72.0 177.5 %all-gather.22.cloned.1.call-start = ((), (), s32[]{:S(2)}) async-start(), calls=%async_computation.8 | async-start | bytes 6291456 | tf_op jit(solution)/shard_map/all_gather | solution.py:50
  106.2 179.4 %all-gather.18.cloned.1.call-start = ((), (), s32[]{:S(2)}) async-start(), calls=%async_computation.6 | async-start | bytes 18874368 | tf_op jit(solution)/shard_map/all_gather | solution.py:50
  190.8 173.8 %reduce-scatter.2.cloned.1.call-start = ((), (), s32[]{:S(2)}) async-start(), calls=%async_computation.4 | async-start | bytes 2359296 | tf_op jit(solution)/shard_map/reduce_scatter | solution.py:107
  255.9 50.7 %copy-start.1 = (bf16[1,1,256,4096]{3,2,1,0:T(8,128)(2,1)S(1)}, bf16[1,1,256,4096]{3,2,1,0:T(8,128)(2,1)}, u32[]{:S(2)}) copy-start(bf16[1,1,256,4096]{3,2,1,0:T(8,128)(2,1)} %all-gather.12.cloned.1.call-done) | copy-start | bytes 6291460
  255.9 50.7 %copy-start.4 = (f32[1,4096]{1,0:T(1,128)S(1)}, f32[1,4096]{1,0:T(1,128)}, u32[]{:S(2)}) copy-start(f32[1,4096]{1,0:T(1,128)} %param.12) | copy-start | bytes 49156
  255.9 50.7 %copy-start.5 = (f32[1,4096]{1,0:T(1,128)S(1)}, f32[1,4096]{1,0:T(1,128)}, u32[]{:S(2)}) copy-start(f32[1,4096]{1,0:T(1,128)} %param.13) | copy-start | bytes 49156
  306.6 8.1 %copy-start.3 = (s32[1,16]{1,0:T(1,128)S(1)}, s32[1,16]{1,0:T(1,128)}, u32[]{:S(2)}) copy-start(s32[1,16]{1,0:T(1,128)} %param.15) | copy-start | bytes 196
  318.7 45.8 %copy-start.2 = (bf16[1,1,256,512]{3,2,1,0:T(8,128)(2,1)S(1)}, bf16[1,1,256,512]{3,2,1,0:T(8,128)(2,1)}, u32[]{:S(2)}) copy-start(bf16[1,1,256,512]{3,2,1,0:T(8,128)(2,1)} %param.9) | copy-start | bytes 786436
  391.2 10.6 %collective-permute-start = (bf16[16,16,512]{2,1,0:T(8,128)(2,1)S(1)}, bf16[16,16,512]{2,1,0:T(8,128)(2,1)S(1)}, u32[]{:S(2)}, u32[]{:S(2)}) collective-permute-start(bf16[16,16,512]{2,1,0:T(8,128)(2,1)S(1)} %all_to_all.5), channel_id=1, source_target_pairs={{0,128},{128,256},{256,384},{384,0},{1,129},{129,257},{257,385},{3... | collective-permute-start | bytes 786440 | tf_op jit(solution)/shard_map/ppermute | solution.py:17
Sparse Core Ops, SparseCore 0:
  9.4 61.9 all-gather.13
  73.5 32.6 all-gather.19
  108.2 71.0 all-gather.15
  181.3 40.0 all-gather.11
  223.3 26.1 all-gather.21
  251.5 34.0 all-gather.17
  323.8 40.7 reduce-scatter.1
